TPU v7x, 128 devices: a whole 4x4x4 slice. The times are simulated.
128 devices in a mesh: expert: 16 (over y, x_lo, core), tensor: 8 (over x_hi, z).
Axes of the slice: x: 4 (x_hi: 2, x_lo: 2; x = x_hi * 2 + x_lo), y: 4, z: 4, core: 2. Of those that a mesh axis runs over, the one named last changes fastest.
Arguments:
- slot_choices: int32 [4096, 4], P('expert'), may hold values from 0 to 31, all different within a row; in each aligned block of 256 rows (0 to 255, 256 to 511, ...) at most 40 rows name the same one
- mix_weights: float32 [4096, 4], P('expert'), may hold values from 0.1 to 2.5
- tokens: bfloat16 [4096, 3584], P('expert'), may hold values from -6 to 6
- cotangent: bfloat16 [4096, 3584], P('expert'), may hold values from -0.71875 to 0.71875
- hot_experts: int32 [2], replicated, may hold values from 0 to 15, as said below
- replica_of: int32 [16], replicated, may hold values from 0 to 15, as said below
- weights_in: bfloat16 [16, 2, 3584, 1024], P('expert', None, None, 'tensor'), may hold values from -0.1796875 to 0.1796875
- weights_down: bfloat16 [16, 1024, 3584], P('expert', 'tensor'), may hold values from -0.1796875 to 0.1796875
- mean_in: bfloat16 [16, 2, 3584, 1024], P('expert', None, None, 'tensor'), may hold values from -1.796875 to 1.796875
- mean_down: bfloat16 [16, 1024, 3584], P('expert', 'tensor'), may hold values from -1.796875 to 1.796875
- square_in: bfloat16 [16, 2, 3584, 1024], P('expert', None, None, 'tensor'), may hold values from 0.099609375 to 1
- square_down: bfloat16 [16, 1024, 3584], P('expert', 'tensor'), may hold values from 0.099609375 to 1
Outputs:
- stepped_in: bfloat16 [16, 2, 3584, 1024], P('expert', None, None, 'tensor')
- stepped_down: bfloat16 [16, 1024, 3584], P('expert', 'tensor')
- averaged_in: bfloat16 [16, 2, 3584, 1024], P('expert', None, None, 'tensor')
- averaged_down: bfloat16 [16, 1024, 3584], P('expert', 'tensor')
- squared_in: bfloat16 [16, 2, 3584, 1024], P('expert', None, None, 'tensor')
- squared_down: bfloat16 [16, 1024, 3584], P('expert', 'tensor')
- copied_in: bfloat16 [16, 2, 3584, 1024], P('expert', None, None, 'tensor')
- copied_down: bfloat16 [16, 1024, 3584], P('expert', 'tensor')
Inputs may be any that keep to these rules, and one draw needn't show every extreme that they name: `slot_choices`: within the 256 tokens of one index of expert, no slot is named by more than 40 choices; the 4 slots of one token differ. `hot_experts`: 2 different experts, one of them expert 16 - 1. `replica_of`: entry j is one of hot_experts and never j; each of hot_experts is named by some entry.
All inputs are finite; a program needn't handle non-finite values.
Results may differ from a plain program's by a relative error of at most 0.023.
Values may be sent and summed in bfloat16 or wider, within the bound.
No kernel may reach another device: no remote copies, remote signals or barrier semaphores. Data moves between devices by JAX's collectives and lax.ppermute only.
A program may use at most 192 MiB of HBM per device.

v0:
```python
import math

import jax
import jax.numpy as jnp
from jax import lax
from jax.sharding import PartitionSpec as P

beta_one = 0.9
beta_two = 0.95
learn_rate = 0.02
decay_rate = 0.1
epsilon = 1e-08
weight_scale = 0.03


def broadcast(block, axis, source):
    block = jnp.where(lax.axis_index(axis) == source, block, jnp.zeros_like(block))
    return lax.psum(block, axis)


def adam_step(weight, moment_one, moment_two, gradient):
    first_new = beta_one * moment_one.astype(jnp.float32) + (1.0 - beta_one) * gradient
    second_new = beta_two * moment_two.astype(jnp.float32) + (1.0 - beta_two) * gradient * gradient
    base_val = weight.astype(jnp.float32)
    weight_new = base_val - learn_rate * (
        first_new / (jnp.sqrt(second_new) + epsilon) + decay_rate * base_val
    )
    return (
        weight_new.astype(jnp.bfloat16),
        first_new.astype(jnp.bfloat16),
        second_new.astype(jnp.bfloat16),
    )


def build_rows(slot_choices, mix_weights, tokens, cotangent, slot_count, capacity, row_count):
    top_count = slot_choices.shape[1]
    flat_ids = slot_choices.reshape(-1)
    entries = flat_ids.shape[0]
    onehot = (flat_ids[:, None] == jnp.arange(slot_count, dtype=jnp.int32)[None, :]).astype(
        jnp.int32
    )
    before = jnp.cumsum(onehot, axis=0) - onehot
    position = jnp.sum(before * onehot, axis=1)
    target = flat_ids * capacity + position
    wanted = (
        jnp.arange(slot_count, dtype=jnp.int32)[:, None] * capacity
        + jnp.arange(row_count, dtype=jnp.int32)[None, :]
    ).reshape(-1)
    matches = wanted[:, None] == target[None, :]
    present = jnp.any(matches, axis=1)
    source = jnp.sum(jnp.where(matches, jnp.arange(entries, dtype=jnp.int32)[None, :], 0), axis=1)
    token_index = source // top_count
    rows_token = jnp.where(present[:, None], tokens[token_index], jnp.zeros((), tokens.dtype))
    weight = jnp.where(present, mix_weights.reshape(-1)[source], 0.0)
    rows_cotan = (weight[:, None] * cotangent[token_index].astype(jnp.float32)).astype(jnp.bfloat16)
    row_shape = (slot_count // 2, 2, row_count, tokens.shape[1])
    return (rows_token.reshape(row_shape), rows_cotan.reshape(row_shape))


def slot_terms(rows_token, rows_cotan, weight_in, weight_down, scale_in, scale_down):
    joined = (
        jnp.einsum("rd,gdf->grf", rows_token, weight_in, preferred_element_type=jnp.float32)
        * scale_in
    )
    gate_val = joined[0]
    up_val = joined[1]
    sigmoid_val = jax.nn.sigmoid(gate_val)
    active = gate_val * sigmoid_val
    hidden = (active * up_val).astype(jnp.bfloat16)
    back_grad = (
        jnp.einsum("rd,fd->rf", rows_cotan, weight_down, preferred_element_type=jnp.float32)
        * scale_down
    )
    slope_gate = (back_grad * up_val * sigmoid_val * (1.0 + gate_val * (1.0 - sigmoid_val))).astype(
        jnp.bfloat16
    )
    slope_up = (back_grad * active).astype(jnp.bfloat16)
    slopes = jnp.stack([slope_gate, slope_up])
    grad_in = jnp.einsum("rd,grf->gdf", rows_token, slopes, preferred_element_type=jnp.float32)
    grad_down = jnp.einsum("rf,rd->fd", hidden, rows_cotan, preferred_element_type=jnp.float32)
    return (grad_in, grad_down)


def body(
    slot_choices,
    mix_weights,
    tokens,
    cotangent,
    hot_experts,
    replica_of,
    weights_in,
    weights_down,
    mean_in,
    mean_down,
    square_in,
    square_down,
):
    expert_count = lax.axis_size("expert")
    tensor_count = lax.axis_size("tensor")
    token_count = slot_choices.shape[0]
    top_count = slot_choices.shape[1]
    share = (5 * token_count * top_count + 8 * expert_count * tensor_count - 1) // (
        8 * expert_count * tensor_count
    )
    capacity = share * tensor_count
    own_index = lax.axis_index("expert")
    my_copy = replica_of[own_index]
    hot_count = hot_experts.shape[0]
    own_in = weights_in[0]
    own_down = weights_down[0]
    width = tokens.shape[1]
    inner = own_in.shape[2]
    scale_in = 1.0 / (weight_scale * math.sqrt(width))
    scale_down = 1.0 / (weight_scale * math.sqrt(inner * tensor_count))
    held = [jnp.zeros_like(weights_in[0]), jnp.zeros_like(weights_down[0])]
    for which in range(hot_count):
        root_id = hot_experts[which]
        arrived = (
            broadcast(weights_in[0], "expert", root_id),
            broadcast(weights_down[0], "expert", root_id),
        )
        chosen = my_copy == root_id
        held = [jnp.where(chosen, incoming, previous) for incoming, previous in zip(arrived, held)]
    weight_sets = ((own_in, own_down), (held[0], held[1]))
    built_token, built_cotan = build_rows(
        slot_choices, mix_weights, tokens, cotangent, 2 * expert_count, capacity, capacity
    )
    recv_token, recv_cotan = (
        lax.all_to_all(built_token, "expert", split_axis=0, concat_axis=0, tiled=True),
        lax.all_to_all(built_cotan, "expert", split_axis=0, concat_axis=0, tiled=True),
    )
    result = []
    for add_which in range(2):
        part_in, part_down = slot_terms(
            recv_token[:, add_which].reshape(-1, width),
            recv_cotan[:, add_which].reshape(-1, width),
            weight_sets[add_which][0],
            weight_sets[add_which][1],
            scale_in,
            scale_down,
        )
        result.append(part_in)
        result.append(part_down)
    totals = tuple(result)
    grad_in = totals[0] * scale_in
    grad_down = totals[1] * scale_down
    copy_in = totals[2] * scale_in
    copy_down = totals[3] * scale_down
    grad_in_low = grad_in.astype(jnp.bfloat16)
    grad_down_low = grad_down.astype(jnp.bfloat16)
    copy_in_low = copy_in.astype(jnp.bfloat16)
    copy_down_low = copy_down.astype(jnp.bfloat16)
    nothing_in = jnp.zeros_like(grad_in_low)
    nothing_down = jnp.zeros_like(grad_down_low)
    total_in = grad_in
    total_down = grad_down
    copy_total_in = jnp.zeros_like(copy_in)
    copy_total_down = jnp.zeros_like(copy_down)
    for which in range(hot_count):
        root_id = hot_experts[which]
        is_owner = own_index == root_id
        chosen = my_copy == root_id
        term_in = jnp.where(is_owner, grad_in_low, jnp.where(chosen, copy_in_low, nothing_in))
        term_down = jnp.where(
            is_owner, grad_down_low, jnp.where(chosen, copy_down_low, nothing_down)
        )
        summed_in, summed_down = (
            lax.psum(term_in, "expert").astype(jnp.float32),
            lax.psum(term_down, "expert").astype(jnp.float32),
        )
        total_in = jnp.where(is_owner, summed_in, total_in)
        total_down = jnp.where(is_owner, summed_down, total_down)
        copy_total_in = jnp.where(chosen, summed_in, copy_total_in)
        copy_total_down = jnp.where(chosen, summed_down, copy_total_down)
    stepped_in, averaged_in, squared_in = adam_step(own_in, mean_in[0], square_in[0], total_in)
    stepped_down, averaged_down, squared_down = adam_step(
        own_down, mean_down[0], square_down[0], total_down
    )
    copied_in = jnp.zeros_like(stepped_in)
    copied_down = jnp.zeros_like(stepped_down)
    for which in range(hot_count):
        root_id = hot_experts[which]
        fresh_in, fresh_down = (
            broadcast(stepped_in, "expert", root_id),
            broadcast(stepped_down, "expert", root_id),
        )
        chosen = my_copy == root_id
        copied_in = jnp.where(chosen, fresh_in, copied_in)
        copied_down = jnp.where(chosen, fresh_down, copied_down)
    return (
        stepped_in[None],
        stepped_down[None],
        averaged_in[None],
        averaged_down[None],
        squared_in[None],
        squared_down[None],
        copied_in[None],
        copied_down[None],
    )


def solution(mesh):
    placed = (
        P("expert", None),
        P("expert", None),
        P("expert", None),
        P("expert", None),
        P(),
        P(),
        P("expert", None, None, "tensor"),
        P("expert", "tensor", None),
        P("expert", None, None, "tensor"),
        P("expert", "tensor", None),
        P("expert", None, None, "tensor"),
        P("expert", "tensor", None),
    )
    return jax.shard_map(
        body,
        mesh=mesh,
        in_specs=placed,
        out_specs=(
            P("expert", None, None, "tensor"),
            P("expert", "tensor", None),
            P("expert", None, None, "tensor"),
            P("expert", "tensor", None),
            P("expert", None, None, "tensor"),
            P("expert", "tensor", None),
            P("expert", None, None, "tensor"),
            P("expert", "tensor", None),
        ),
        check_vma=False,
    )
```

profile of v0, /device:TPU:1, one launch (start us, length us, event | category | flops | bytes accessed | tf_op | source)
XLA Modules:
  0.0 698.7 jit_solution(2604066244204291419)
XLA Ops:
  7.2 0.9 copy.69
  8.4 9.0 %reduce-window.6 = s32[32,8,128]{2,1,0:T(8,128)S(1)} reduce-window(s32[32,8,128]{2,1,0:T(8,128)S(1)} %fusion.80, s32[]{:T(128)} %constant.27.clone.1), window={size=1x1x128 pad=0_0x0_0x127_0}, to_apply=%region_0.1 | reduce-window | flops 4161536 | bytes 262148 | tf_op jit(solution)/shard_map/reduce-window
  18.1 0.8 fusion.2
  18.9 0.8 compare_reduce_fusion
  19.9 8.0 %gather_fusion.2 = bf16[1280,3584]{1,0:T(8,128)(2,1)} fusion(bf16[256,3584]{1,0:T(8,128)(2,1)S(1)} %copy-done, s32[2048]{0:T(1024)S(1)} %get-tuple-element.82), kind=kCustom, calls=%fused_computation.2 | custom fusion | bytes 18355200 | tf_op jit(solution)/shard_map/gather | solution.py:53
  27.9 7.9 %broadcast_select_fusion = bf16[16,2,40,3584]{3,2,1,0:T(8,128)(2,1)} fusion(bf16[16,2,40,3584]{3,2,1,0:T(8,128)(2,1)} %bitcast.210, pred[16,2,40]{2,1,0:T(4,128)(4,1)S(1)} %reduce_or.12), kind=kLoop, calls=%fused_computation.5 | loop fusion | flops 4587520 | bytes 18351360 | tf_op jit(solution)/shard_map/jit(_where)/select_n | solution.py:53
  35.8 7.0 %all-to-all-start.1 = ((bf16[16,2,40,3584]{3,2,1,0:T(8,128)(2,1)}), bf16[16,2,40,3584]{3,2,1,0:T(8,128)(2,1)}, u32[]{:S(2)}, u32[]{:S(2)}) async-start(bf16[16,2,40,3584]{3,2,1,0:T(8,128)(2,1)} %broadcast_select_fusion), calls=%async_computation.1 | async-start | bytes 18350080 | tf_op jit(solution)/shard_map/all_to_all | solution.py:129
  43.1 5.0 gather_fusion
  48.2 7.8 %gather_fusion.1 = bf16[1280,3584]{1,0:T(8,128)(2,1)} fusion(bf16[256,3584]{1,0:T(8,128)(2,1)S(1)} %copy-done.2, s32[2048]{0:T(1024)S(1)} %get-tuple-element.82), kind=kCustom, calls=%fused_computation.1 | custom fusion | bytes 18355200 | tf_op jit(solution)/shard_map/gather | solution.py:55
  56.1 10.6 %fusion = bf16[16,2,40,3584]{3,2,1,0:T(8,128)(2,1)} fusion(bf16[16,2,40,3584]{3,2,1,0:T(8,128)(2,1)} %bitcast.209, f32[16,2,40]{2,1,0:T(2,128)S(1)} %broadcast_select_fusion.5), kind=kLoop, calls=%fused_computation.4 | loop fusion | flops 13762560 | bytes 18355200 | tf_op jit(solution)/shard_map/convert_element_type | solution.py:55
  66.6 79.1 %all-to-all-done.1 = bf16[16,2,40,3584]{3,2,1,0:T(8,128)(2,1)} async-done(((bf16[16,2,40,3584]{3,2,1,0:T(8,128)(2,1)}), bf16[16,2,40,3584]{3,2,1,0:T(8,128)(2,1)}, u32[]{:S(2)}, u32[]{:S(2)}) %all-to-all-start.1) | async-done | bytes 9175072 | tf_op jit(solution)/shard_map/all_to_all | solution.py:129
  145.7 5.5 all-to-all-start
  151.3 0.6 fusion.93
  153.2 2.8 copy.67
  156.0 1.3 bitcast_select_fusion.4
  157.4 2.1 bitcast_select_fusion.3
  163.3 6.6 fusion.92
  169.9 2.1 copy-done.3
  172.0 2.2 fusion.27
  174.2 146.3 %all-to-all-done = bf16[16,2,40,3584]{3,2,1,0:T(8,128)(2,1)} async-done(((bf16[16,2,40,3584]{3,2,1,0:T(8,128)(2,1)}), bf16[16,2,40,3584]{3,2,1,0:T(8,128)(2,1)}, u32[]{:S(2)}, u32[]{:S(2)}) %all-to-all-start) | async-done | bytes 9175072 | tf_op jit(solution)/shard_map/all_to_all | solution.py:130
  320.5 6.6 fusion.91
  327.1 2.2 convolution_multiply_fusion.3
  329.3 1.4 fusion.75
  330.6 34.2 %all-reduce.11.cloned.1.call-done = (bf16[128,3584]{1,0:T(8,128)(2,1)}, bf16[128,3584]{1,0:T(8,128)(2,1)}, bf16[2,3584,128]{1,2,0:T(8,128)(2,1)}, bf16[2,3584,128]{1,2,0:T(8,128)(2,1)}) async-done(((bf16[128,3584]{1,0:T(8,128)(2,1)}, bf16[128,3584]{1,0:T(8,128)(2,1)}, bf16[2,3584,128]{1,2,0:T(8,128)(2,1)}, bf16[2,3584,128]{1,2,0:T(8,128)(2,1)}), (bf16[128,3584]{1,0:T(8,128)(2,1)}, ...) | async-done | bytes 5505040 | tf_op jit(solution)/shard_map/psum | solution.py:18
  364.8 4.4 fusion.33
  369.4 2.2 select_select_fusion.3
  371.6 1.4 fusion.76
  373.0 1.3 slice-done
  374.3 1.6 fusion.1
  375.9 3.6 bitcast_select_fusion.1
  379.9 3.8 copy.68
  383.7 3.8 copy.78
  387.5 136.6 %all-reduce.9.cloned.1.call-done = (bf16[2,3584,128]{1,2,0:T(8,128)(2,1)}, bf16[2,3584,128]{1,2,0:T(8,128)(2,1)}, bf16[128,3584]{1,0:T(8,128)(2,1)}, bf16[128,3584]{1,0:T(8,128)(2,1)}) async-done(((bf16[2,3584,128]{1,2,0:T(8,128)(2,1)}, bf16[2,3584,128]{1,2,0:T(8,128)(2,1)}, bf16[128,3584]{1,0:T(8,128)(2,1)}, bf16[128,3584]{1,0:T(8,128)(2,1)}), (bf16[2,3584,128]{1,2,0:T(8,128)(2,1)}, ...) | async-done | bytes 5505040 | tf_op jit(solution)/shard_map/psum | solution.py:168
  524.1 6.0 broadcast_select_fusion.3
  530.1 1.0 broadcast_select_fusion.4
  531.4 0.9 copy-done.4
  532.3 5.2 broadcast_select_fusion.1
  537.5 1.6 broadcast_select_fusion.2
  539.4 1.5 copy-done.5
  540.9 5.6 fusion.11
  546.5 3.8 copy.80
  550.3 3.9 copy.81
  554.2 2.2 copy.79
  556.5 3.6 fusion.38
  560.1 123.0 %all-reduce.7.cloned.1.call-done = (bf16[2,3584,128]{1,2,0:T(8,128)(2,1)}, bf16[2,3584,128]{1,2,0:T(8,128)(2,1)}, bf16[128,3584]{1,0:T(8,128)(2,1)}, bf16[128,3584]{1,0:T(8,128)(2,1)}) async-done(((bf16[2,3584,128]{1,2,0:T(8,128)(2,1)}, bf16[2,3584,128]{1,2,0:T(8,128)(2,1)}, bf16[128,3584]{1,0:T(8,128)(2,1)}, bf16[128,3584]{1,0:T(8,128)(2,1)}), (bf16[2,3584,128]{1,2,0:T(8,128)(2,1)}, ...) | async-done | bytes 5505040 | tf_op jit(solution)/shard_map/psum | solution.py:18
  683.1 2.9 select_bitcast_fusion
  686.0 3.9 copy.82
  690.0 2.2 select_bitcast_fusion.1
  (89 shorter events, 3.7 us)
Async XLA Ops:
  7.2 12.7 %copy-start = (bf16[256,3584]{1,0:T(8,128)(2,1)S(1)}, bf16[256,3584]{1,0:T(8,128)(2,1)}, u32[]{:S(2)}) copy-start(bf16[256,3584]{1,0:T(8,128)(2,1)} %param.14) | copy-start | bytes 5505028
  35.8 7.0 %copy-start.20 = (f32[256,4]{0,1:T(4,128)S(1)}, f32[256,4]{0,1:T(4,128)}, u32[]{:S(2)}) copy-start(f32[256,4]{0,1:T(4,128)} %param.13) | copy-start | bytes 12292
  35.8 109.9 %all-to-all-start.1 = ((bf16[16,2,40,3584]{3,2,1,0:T(8,128)(2,1)}), bf16[16,2,40,3584]{3,2,1,0:T(8,128)(2,1)}, u32[]{:S(2)}, u32[]{:S(2)}) async-start(bf16[16,2,40,3584]{3,2,1,0:T(8,128)(2,1)} %broadcast_select_fusion), calls=%async_computation.1 | async-start | bytes 18350080 | tf_op jit(solution)/shard_map/all_to_all | solution.py:129
  43.1 5.1 copy-start.2
  66.6 84.7 %copy-start.21 = (s32[2]{0:T(128)S(1)}, s32[2]{0:T(128)}, u32[]{:S(2)}) copy-start(s32[2]{0:T(128)} %param.16) | copy-start | bytes 28
  145.7 174.8 %all-to-all-start = ((bf16[16,2,40,3584]{3,2,1,0:T(8,128)(2,1)}), bf16[16,2,40,3584]{3,2,1,0:T(8,128)(2,1)}, u32[]{:S(2)}, u32[]{:S(2)}) async-start(bf16[16,2,40,3584]{3,2,1,0:T(8,128)(2,1)} %fusion), calls=%async_computation | async-start | bytes 18350080 | tf_op jit(solution)/shard_map/all_to_all | solution.py:130
  151.2 213.6 %all-reduce.11.cloned.1.call-start = ((), (), s32[]{:S(2)}) async-start(), calls=%async_computation.4 | async-start | bytes 11010048 | tf_op jit(solution)/shard_map/psum | solution.py:18
  153.2 2.9 copy-start.12
  159.5 0.7 copy-start.24
  159.5 364.6 %all-reduce.9.cloned.1.call-start = ((), (), s32[]{:S(2)}) async-start(), calls=%async_computation.3 | async-start | bytes 11010048 | tf_op jit(solution)/shard_map/psum | solution.py:168
  163.3 8.7 %copy-start.17 = (bf16[1,2,3584,128]{3,2,1,0:T(8,128)(2,1)S(1)}, bf16[1,2,3584,128]{3,2,1,0:T(8,128)(2,1)}, u32[]{:S(2)}) copy-start(bf16[1,2,3584,128]{3,2,1,0:T(8,128)(2,1)} %param.18) | copy-start | bytes 5505028
  169.9 2.1 copy-start.3
  320.5 6.6 copy-start.19
  329.3 39.9 %slice-start.4 = ((s8[4587520]{0:T(1024)(128)(4,1)}), s8[393216]{0:T(1024)(128)(4,1)S(1)}, s32[]{:S(2)}) async-start(s8[4587520]{0:T(1024)(128)(4,1)} %bitcast.222), calls=%async_computation.9 | async-start | bytes 786432
  364.8 4.4 copy-start.11
  364.8 4.6 slice-start.5
  369.4 2.2 copy-start.22
  369.4 2.2 copy-start.23
  369.4 6.5 slice-start.2
  371.6 2.7 slice-start
  371.6 2.6 slice-start.1
  371.6 4.3 slice-start.3
  375.9 3.7 copy-start.9
  379.6 303.5 %all-reduce.7.cloned.1.call-start = ((), (), s32[]{:S(2)}) async-start(), calls=%async_computation.2 | async-start | bytes 11010048 | tf_op jit(solution)/shard_map/psum | solution.py:18
  524.1 7.2 %copy-start.6 = (bf16[1,2,3584,128]{2,3,1,0:T(8,128)(2,1)S(1)}, bf16[1,2,3584,128]{2,3,1,0:T(8,128)(2,1)}, u32[]{:S(2)}) copy-start(bf16[1,2,3584,128]{2,3,1,0:T(8,128)(2,1)} %copy.78) | copy-start | bytes 5505028
  524.1 7.2 %copy-start.10 = (f32[2,3584,128]{1,2,0:T(8,128)S(1)}, f32[2,3584,128]{1,2,0:T(8,128)}, u32[]{:S(2)}) copy-start(f32[2,3584,128]{1,2,0:T(8,128)} %copy-done.9) | copy-start | bytes 11010052
  524.1 7.2 %copy-start.15 = (bf16[2,3584,128]{1,2,0:T(8,128)(2,1)S(1)}, bf16[2,3584,128]{1,2,0:T(8,128)(2,1)}, u32[]{:S(2)}) copy-start(bf16[2,3584,128]{1,2,0:T(8,128)(2,1)} %get-tuple-element.46) | copy-start | bytes 5505028
  524.1 7.2 %copy-start.16 = (bf16[2,3584,128]{1,2,0:T(8,128)(2,1)S(1)}, bf16[2,3584,128]{1,2,0:T(8,128)(2,1)}, u32[]{:S(2)}) copy-start(bf16[2,3584,128]{1,2,0:T(8,128)(2,1)} %get-tuple-element.47) | copy-start | bytes 5505028
  530.1 1.2 copy-start.13
  530.1 2.2 copy-start.4
  537.5 1.8 copy-start.7
  539.4 1.5 copy-start.5
  550.3 3.9 copy-start.8
  554.2 2.3 copy-start.14
  686.0 4.0 copy-start.18
  686.0 6.2 copy-start.1
Sparse Core Ops, SparseCore 0:
  159.6 205.1 all-reduce.10
  379.7 144.3 all-reduce.8
  539.5 143.4 all-reduce.6
where the time goes:
time: 700 us; the launch traced here: 699 us
  waiting for transfers between devices  519 us (74%)
  local copies, waits for them, and re-layouts  68.5 us (10%)
  other arithmetic  61.1 us (9%)
  matrix products  18.9 us (3%)
  between operations  18 us (3%)
  starting transfers between devices  13 us (2%)
    psum x2, waiting for transfers between devices, broadcast(): return lax.psum(block, axis)  157 us
    all_to_all x1, waiting for transfers between devices, body(): lax.all_to_all(built_cotan, 'expert', split_axis=0, concat_axis=0, tiled=...  146 us
    psum x1, waiting for transfers between devices, body(): lax.psum(term_in, 'expert').astype(jnp.float32)  137 us
    all_to_all x1, waiting for transfers between devices, body(): lax.all_to_all(built_token, 'expert', split_axis=0, concat_axis=0, tiled=...  79.1 us
    unnamed x71, local copies, waits for them, and re-layouts  32.5 us
    select_n x6, other arithmetic, broadcast(): jnp.where(lax.axis_index(axis) == source, block, jnp.zeros_like(block))  17.2 us
  transfers between devices with their start and end apart: 5, of which 5 were waited for; matrix products, arithmetic and copies ran while one was open for 11% of the time, Pallas kernels for 0%

commit v1 on v0

--- a/solution.py
+++ b/solution.py
@@ -79,6 +79,39 @@
     grad_in = jnp.einsum("rd,grf->gdf", rows_token, slopes, preferred_element_type=jnp.float32)
     grad_down = jnp.einsum("rf,rd->fd", hidden, rows_cotan, preferred_element_type=jnp.float32)
     return (grad_in, grad_down)
+
+
+def pack(part_in, part_down, groups):
+    width = part_in.shape[1]
+    inner = part_in.shape[2]
+    return jnp.concatenate(
+        [
+            part_in.reshape(groups, 2 * width // groups, inner),
+            part_down.reshape(groups, width // groups, inner),
+        ],
+        axis=1,
+    )
+
+
+def unpack(packed, width, inner):
+    groups = packed.shape[0]
+    split = 2 * width // groups
+    part_in = packed[:, :split].reshape(2, width, inner)
+    part_down = packed[:, split:].reshape(inner, width)
+    return part_in, part_down
+
+
+def exchange(block):
+    return lax.all_to_all(block, "expert", 0, 0, tiled=True)
+
+
+def spread_hot(packed, hot_experts, replica_of):
+    arrived = exchange(packed)
+    first = lax.dynamic_index_in_dim(arrived, hot_experts[0], 0, keepdims=False)
+    second = lax.dynamic_index_in_dim(arrived, hot_experts[1], 0, keepdims=False)
+    wants_first = (replica_of == hot_experts[0])[:, None, None]
+    outgoing = jnp.where(wants_first, first[None], second[None])
+    return exchange(outgoing)
 
 
 def body(
@@ -104,24 +137,16 @@
     )
     capacity = share * tensor_count
     own_index = lax.axis_index("expert")
-    my_copy = replica_of[own_index]
-    hot_count = hot_experts.shape[0]
     own_in = weights_in[0]
     own_down = weights_down[0]
     width = tokens.shape[1]
     inner = own_in.shape[2]
     scale_in = 1.0 / (weight_scale * math.sqrt(width))
     scale_down = 1.0 / (weight_scale * math.sqrt(inner * tensor_count))
-    held = [jnp.zeros_like(weights_in[0]), jnp.zeros_like(weights_down[0])]
-    for which in range(hot_count):
-        root_id = hot_experts[which]
-        arrived = (
-            broadcast(weights_in[0], "expert", root_id),
-            broadcast(weights_down[0], "expert", root_id),
-        )
-        chosen = my_copy == root_id
-        held = [jnp.where(chosen, incoming, previous) for incoming, previous in zip(arrived, held)]
-    weight_sets = ((own_in, own_down), (held[0], held[1]))
+    held_in, held_down = unpack(
+        spread_hot(pack(own_in, own_down, expert_count), hot_experts, replica_of), width, inner
+    )
+    weight_sets = ((own_in, own_down), (held_in, held_down))
     built_token, built_cotan = build_rows(
         slot_choices, mix_weights, tokens, cotangent, 2 * expert_count, capacity, capacity
     )
@@ -146,47 +171,39 @@
     grad_down = totals[1] * scale_down
     copy_in = totals[2] * scale_in
     copy_down = totals[3] * scale_down
-    grad_in_low = grad_in.astype(jnp.bfloat16)
-    grad_down_low = grad_down.astype(jnp.bfloat16)
-    copy_in_low = copy_in.astype(jnp.bfloat16)
-    copy_down_low = copy_down.astype(jnp.bfloat16)
-    nothing_in = jnp.zeros_like(grad_in_low)
-    nothing_down = jnp.zeros_like(grad_down_low)
-    total_in = grad_in
-    total_down = grad_down
-    copy_total_in = jnp.zeros_like(copy_in)
-    copy_total_down = jnp.zeros_like(copy_down)
-    for which in range(hot_count):
-        root_id = hot_experts[which]
-        is_owner = own_index == root_id
-        chosen = my_copy == root_id
-        term_in = jnp.where(is_owner, grad_in_low, jnp.where(chosen, copy_in_low, nothing_in))
-        term_down = jnp.where(
-            is_owner, grad_down_low, jnp.where(chosen, copy_down_low, nothing_down)
-        )
-        summed_in, summed_down = (
-            lax.psum(term_in, "expert").astype(jnp.float32),
-            lax.psum(term_down, "expert").astype(jnp.float32),
-        )
-        total_in = jnp.where(is_owner, summed_in, total_in)
-        total_down = jnp.where(is_owner, summed_down, total_down)
-        copy_total_in = jnp.where(chosen, summed_in, copy_total_in)
-        copy_total_down = jnp.where(chosen, summed_down, copy_total_down)
+    copy_packed = pack(
+        copy_in.astype(jnp.bfloat16), copy_down.astype(jnp.bfloat16), expert_count
+    )
+    arrived = exchange(copy_packed).astype(jnp.float32)
+    sources = jnp.arange(expert_count, dtype=jnp.int32)
+    sums = []
+    for which in range(2):
+        picked = (replica_of == hot_experts[which])[:, None, None]
+        sums.append(jnp.sum(jnp.where(picked, arrived, 0.0), axis=0))
+    to_owner = jnp.where(
+        (sources == hot_experts[0])[:, None, None],
+        sums[0][None],
+        jnp.where((sources == hot_experts[1])[:, None, None], sums[1][None], 0.0),
+    ).astype(jnp.bfloat16)
+    gathered_in, gathered_down = unpack(
+        exchange(to_owner).astype(jnp.float32), width, inner
+    )
+    is_hot = jnp.any(hot_experts == own_index)
+    total_in = jnp.where(
+        is_hot, grad_in.astype(jnp.bfloat16).astype(jnp.float32) + gathered_in, grad_in
+    )
+    total_down = jnp.where(
+        is_hot, grad_down.astype(jnp.bfloat16).astype(jnp.float32) + gathered_down, grad_down
+    )
     stepped_in, averaged_in, squared_in = adam_step(own_in, mean_in[0], square_in[0], total_in)
     stepped_down, averaged_down, squared_down = adam_step(
         own_down, mean_down[0], square_down[0], total_down
     )
-    copied_in = jnp.zeros_like(stepped_in)
-    copied_down = jnp.zeros_like(stepped_down)
-    for which in range(hot_count):
-        root_id = hot_experts[which]
-        fresh_in, fresh_down = (
-            broadcast(stepped_in, "expert", root_id),
-            broadcast(stepped_down, "expert", root_id),
-        )
-        chosen = my_copy == root_id
-        copied_in = jnp.where(chosen, fresh_in, copied_in)
-        copied_down = jnp.where(chosen, fresh_down, copied_down)
+    copied_in, copied_down = unpack(
+        spread_hot(pack(stepped_in, stepped_down, expert_count), hot_experts, replica_of),
+        width,
+        inner,
+    )
     return (
         stepped_in[None],
         stepped_down[None],

time: 700 us -> 531 us (0.76)
  waiting for transfers between devices: 519 us -> 277 us
  blocking collectives: 0 us -> 37.9 us
  starting transfers between devices: 13 us -> 38.6 us
  local copies, waits for them, and re-layouts: 68.5 us -> 91.3 us
  between operations: 18 us -> 4.86 us
  other arithmetic: 61.1 us -> 49.6 us
  matrix products: 18.9 us -> 29.8 us
    psum x3 -> x0, waiting for transfers between devices: 294 us -> none  [the longest x2 157 us: broadcast(): return lax.psum(block, axis)]
    all_to_all x0 -> x5, waiting for transfers between devices: none -> 110 us  [exchange(): return lax.all_to_all(block, 'expert', 0, 0, tiled=True)]
    all_to_all x1, waiting for transfers between devices: 146 us -> 88.2 us  [body(): lax.all_to_all(built_cotan, 'expert', split_axis=0, concat_axis=0, tiled=...]
    all_to_all x0 -> x1, blocking collectives: none -> 37.9 us  [exchange(): return lax.all_to_all(block, 'expert', 0, 0, tiled=True)]
    all_to_all x0 -> x5, starting transfers between devices: none -> 27.5 us  [exchange(): return lax.all_to_all(block, 'expert', 0, 0, tiled=True)]
    broadcast_in_dim x4 -> x0, other arithmetic: 14.4 us -> none  [the longest x1 5.64 us: body(): squared_in[None]]
    select_n x6 -> x2, other arithmetic: 17.2 us -> 3.68 us  [spread_hot(): outgoing = jnp.where(wants_first, first[None], second[None])]
    slice x3 -> x9, local copies, waits for them, and re-layouts: 0.8 us -> 13 us  [the longest x3 8.21 us: unpack(): part_in = packed[:, :split].reshape(2, width, inner)]
  transfers between devices with their start and end apart: 5 -> 7, of which waited for: 5 -> 7; matrix products, arithmetic and copies ran while one was open for 11% -> 17% of each run, Pallas kernels for 0% -> 0%
where the time goes in v1:
time: 531 us; the launch traced here: 529 us
  waiting for transfers between devices  277 us (52%)
  local copies, waits for them, and re-layouts  91.3 us (17%)
  other arithmetic  49.6 us (9%)
  starting transfers between devices  38.6 us (7%)
  blocking collectives  37.9 us (7%)
  matrix products  29.8 us (6%)
    all_to_all x5, waiting for transfers between devices, exchange(): return lax.all_to_all(block, 'expert', 0, 0, tiled=True)  110 us
    all_to_all x1, waiting for transfers between devices, body(): lax.all_to_all(built_cotan, 'expert', split_axis=0, concat_axis=0, tiled=...  88.2 us
    all_to_all x1, waiting for transfers between devices, body(): lax.all_to_all(built_token, 'expert', split_axis=0, concat_axis=0, tiled=...  79.3 us
    all_to_all x1, blocking collectives, exchange(): return lax.all_to_all(block, 'expert', 0, 0, tiled=True)  37.9 us
    all_to_all x5, starting transfers between devices, exchange(): return lax.all_to_all(block, 'expert', 0, 0, tiled=True)  27.5 us
    unnamed x48, local copies, waits for them, and re-layouts  22.3 us
    dot_general x2, matrix products, slot_terms(): jnp.einsum('rd,grf->gdf', rows_token, slopes, preferred_element_type=jnp....  12.4 us
  transfers between devices with their start and end apart: 7, of which 7 were waited for; matrix products, arithmetic and copies ran while one was open for 17% of the time, Pallas kernels for 0%

profile of v1, /device:TPU:1, one launch (start us, length us, event | category | flops | bytes accessed | tf_op | source)
XLA Modules:
  0.0 529.5 jit_solution(8380408574677888426)
XLA Ops:
  0.6 2.4 reshape_squeeze.22
  3.1 3.3 pad_maximum_fusion
  6.3 7.0 %all-to-all-start.2 = ((bf16[16,672,128]{2,1,0:T(8,128)(2,1)}), bf16[16,672,128]{2,1,0:T(8,128)(2,1)}, u32[]{:S(2)}, u32[]{:S(2)}) async-start(bf16[16,672,128]{2,1,0:T(8,128)(2,1)} %pad_maximum_fusion), calls=%async_computation.2 | async-start | bytes 5505024 | tf_op jit(solution)/shard_map/all_to_all | solution.py:105
  19.5 28.0 %all-to-all-done.2 = bf16[16,672,128]{2,1,0:T(8,128)(2,1)} async-done(((bf16[16,672,128]{2,1,0:T(8,128)(2,1)}), bf16[16,672,128]{2,1,0:T(8,128)(2,1)}, u32[]{:S(2)}, u32[]{:S(2)}) %all-to-all-start.2) | async-done | bytes 2752544 | tf_op jit(solution)/shard_map/all_to_all | solution.py:105
  50.3 5.2 all-to-all-start.3
  55.6 9.0 %reduce-window.6 = s32[32,8,128]{2,1,0:T(8,128)S(1)} reduce-window(s32[32,8,128]{2,1,0:T(8,128)S(1)} %fusion.67, s32[]{:T(128)} %constant.28.clone.1), window={size=1x1x128 pad=0_0x0_0x127_0}, to_apply=%region_1.2 | reduce-window | flops 4161536 | bytes 262148 | tf_op jit(solution)/shard_map/reduce-window
  67.1 7.9 %gather_fusion.2 = bf16[1280,3584]{1,0:T(8,128)(2,1)} fusion(bf16[256,3584]{1,0:T(8,128)(2,1)S(1)} %copy-done, s32[2048]{0:T(1024)S(1)} %get-tuple-element.66), kind=kCustom, calls=%fused_computation.2 | custom fusion | bytes 18355200 | tf_op jit(solution)/shard_map/gather | solution.py:53
  75.0 7.9 %broadcast_select_fusion = bf16[16,2,40,3584]{3,2,1,0:T(8,128)(2,1)} fusion(bf16[16,2,40,3584]{3,2,1,0:T(8,128)(2,1)} %bitcast.213, pred[16,2,40]{2,1,0:T(4,128)(4,1)S(1)} %reduce_or.22), kind=kLoop, calls=%fused_computation.5 | loop fusion | flops 4587520 | bytes 18351360 | tf_op jit(solution)/shard_map/jit(_where)/select_n | solution.py:53
  82.9 6.7 %all-to-all-done.3 = bf16[16,672,128]{2,1,0:T(8,128)(2,1)} async-done(((bf16[16,672,128]{2,1,0:T(8,128)(2,1)}), bf16[16,672,128]{2,1,0:T(8,128)(2,1)}, u32[]{:S(2)}, u32[]{:S(2)}) %all-to-all-start.3) | async-done | bytes 2752544 | tf_op jit(solution)/shard_map/all_to_all | solution.py:105
  89.6 5.5 %all-to-all-start.1 = ((bf16[16,2,40,3584]{3,2,1,0:T(8,128)(2,1)}), bf16[16,2,40,3584]{3,2,1,0:T(8,128)(2,1)}, u32[]{:S(2)}, u32[]{:S(2)}) async-start(bf16[16,2,40,3584]{3,2,1,0:T(8,128)(2,1)} %broadcast_select_fusion), calls=%async_computation.1 | async-start | bytes 18350080 | tf_op jit(solution)/shard_map/all_to_all | solution.py:154
  95.4 5.0 gather_fusion
  100.4 7.8 %gather_fusion.1 = bf16[1280,3584]{1,0:T(8,128)(2,1)} fusion(bf16[256,3584]{1,0:T(8,128)(2,1)S(1)} %copy-done.2, s32[2048]{0:T(1024)S(1)} %get-tuple-element.66), kind=kCustom, calls=%fused_computation.1 | custom fusion | bytes 18355200 | tf_op jit(solution)/shard_map/gather | solution.py:55
  108.2 10.5 %fusion = bf16[16,2,40,3584]{3,2,1,0:T(8,128)(2,1)} fusion(bf16[16,2,40,3584]{3,2,1,0:T(8,128)(2,1)} %bitcast.212, f32[16,2,40]{2,1,0:T(2,128)S(1)} %broadcast_select_fusion.3), kind=kLoop, calls=%fused_computation.4 | loop fusion | flops 13762560 | bytes 18355200 | tf_op jit(solution)/shard_map/convert_element_type | solution.py:55
  118.8 79.3 %all-to-all-done.1 = bf16[16,2,40,3584]{3,2,1,0:T(8,128)(2,1)} async-done(((bf16[16,2,40,3584]{3,2,1,0:T(8,128)(2,1)}), bf16[16,2,40,3584]{3,2,1,0:T(8,128)(2,1)}, u32[]{:S(2)}, u32[]{:S(2)}) %all-to-all-start.1) | async-done | bytes 9175072 | tf_op jit(solution)/shard_map/all_to_all | solution.py:154
  198.1 5.6 %all-to-all-start = ((bf16[16,2,40,3584]{3,2,1,0:T(8,128)(2,1)}), bf16[16,2,40,3584]{3,2,1,0:T(8,128)(2,1)}, u32[]{:S(2)}, u32[]{:S(2)}) async-start(bf16[16,2,40,3584]{3,2,1,0:T(8,128)(2,1)} %fusion), calls=%async_computation | async-start | bytes 18350080 | tf_op jit(solution)/shard_map/all_to_all | solution.py:155
  205.0 1.9 reshape.211
  208.5 6.5 %fusion.75 = (bf16[16,1,40,3584]{3,2,1,0:T(8,128)(2,1)}, bf16[16,1,40,3584]{3,2,1,0:T(8,128)(2,1)S(1)}) fusion(bf16[16,2,40,3584]{3,2,1,0:T(8,128)(2,1)} %all-to-all-done.1), kind=kLoop, calls=%fused_computation.138 | loop fusion | bytes 18350080 | tf_op jit(solution)/shard_map/slice | solution.py:160
  215.0 2.1 copy-done.3
  218.5 88.2 %all-to-all-done = bf16[16,2,40,3584]{3,2,1,0:T(8,128)(2,1)} async-done(((bf16[16,2,40,3584]{3,2,1,0:T(8,128)(2,1)}), bf16[16,2,40,3584]{3,2,1,0:T(8,128)(2,1)}, u32[]{:S(2)}, u32[]{:S(2)}) %all-to-all-start) | async-done | bytes 9175072 | tf_op jit(solution)/shard_map/all_to_all | solution.py:155
  306.7 6.4 %fusion.74 = (bf16[16,1,40,3584]{3,2,1,0:T(8,128)(2,1)}, bf16[16,1,40,3584]{3,2,1,0:T(8,128)(2,1)S(1)}) fusion(bf16[16,2,40,3584]{3,2,1,0:T(8,128)(2,1)} %all-to-all-done), kind=kLoop, calls=%fused_computation.137 | loop fusion | bytes 18350080 | tf_op jit(solution)/shard_map/slice | solution.py:161
  317.4 2.3 copy.84
  319.7 2.1 reshape.214
  321.8 3.0 pad_maximum_fusion.1
  324.7 5.2 all-to-all-start.4
  331.2 32.9 %all-to-all-done.4 = bf16[16,672,128]{2,1,0:T(8,128)(2,1)} async-done(((bf16[16,672,128]{2,1,0:T(8,128)(2,1)}), bf16[16,672,128]{2,1,0:T(8,128)(2,1)}, u32[]{:S(2)}, u32[]{:S(2)}) %all-to-all-start.4) | async-done | bytes 2752544 | tf_op jit(solution)/shard_map/all_to_all | solution.py:105
  364.1 3.0 fusion.1
  367.0 2.4 select_convert_fusion
  369.4 5.3 all-to-all-start.5
  374.7 2.4 copy.72
  377.2 3.8 copy.73
  381.0 3.9 copy.86
  385.5 3.8 fusion.25
  390.2 2.0 fusion.62
  392.2 16.7 %all-to-all-done.5 = bf16[16,672,128]{2,1,0:T(8,128)(2,1)} async-done(((bf16[16,672,128]{2,1,0:T(8,128)(2,1)}), bf16[16,672,128]{2,1,0:T(8,128)(2,1)}, u32[]{:S(2)}, u32[]{:S(2)}) %all-to-all-start.5) | async-done | bytes 2752544 | tf_op jit(solution)/shard_map/all_to_all | solution.py:105
  411.8 7.9 %fusion.31 = (bf16[1,128,3584]{2,1,0:T(8,128)(2,1)}, bf16[128,3584]{1,0:T(8,128)(2,1)S(1)}, bf16[1,128,3584]{2,1,0:T(8,128)(2,1)}) fusion(bf16[1,128,3584]{2,1,0:T(8,128)(2,1)} %param.23, bf16[1,128,3584]{2,1,0:T(8,128)(2,1)} %param.21, bf16[1,128,3584]{2,1,0:T(8,128)(2,1)S(1)} %copy-done.7, f32[128,3584]{1,0:T(8,128)} %reshape.216, ...), kind=kOutput, calls=%fused_computation.59 | convolution fusion | flops 598704128 | bytes 12582913 | tf_op jit(solution)/shard_map/rf,rd->fd/dot_general | solution.py:80
  420.8 3.7 slice.98
  424.5 5.2 copy.85
  429.7 10.8 %fusion.14 = (bf16[1,2,3584,128]{2,3,1,0:T(8,128)(2,1)}, bf16[2,3584,128]{1,2,0:T(8,128)(2,1)S(1)}, bf16[1,2,3584,128]{2,3,1,0:T(8,128)(2,1)}) fusion(bf16[1,2,3584,128]{2,3,1,0:T(8,128)(2,1)} %copy.86, bf16[1,2,3584,128]{2,3,1,0:T(8,128)(2,1)} %copy.73, bf16[1,2,3584,128]{2,3,1,0:T(8,128)(2,1)} %copy.72, f32[2,3584,128]{1,2,0:T(8,128)} %copy.85, ...), kind=kOutput, calls=%fused_computation.41 | convolution fusion | flops 1196589056 | bytes 19595264 | tf_op jit(solution)/shard_map/rd,grf->gdf/dot_general | solution.py:79
  440.5 2.2 copy.87
  444.4 37.9 %all_to_all.40 = bf16[16,672,128]{2,1,0:T(8,128)(2,1)S(1)} all-to-all(bf16[16,672,128]{2,1,0:T(8,128)(2,1)S(1)} %pad_maximum_fusion.2), channel_id=1, replica_groups=mesh['expert'=16,'tensor'=8] {'expert'}, dimensions={0} | all-to-all | bytes 5505024 | tf_op jit(solution)/shard_map/all_to_all | solution.py:105
  482.4 1.9 broadcast_select_fusion.1
  484.3 4.8 all-to-all-start.7
  489.1 2.3 copy.88
  491.4 3.9 copy.89
  495.3 2.2 copy.90
  497.6 25.7 %all-to-all-done.7 = bf16[16,672,128]{2,1,0:T(8,128)(2,1)} async-done(((bf16[16,672,128]{2,1,0:T(8,128)(2,1)}), bf16[16,672,128]{2,1,0:T(8,128)(2,1)}, u32[]{:S(2)}, u32[]{:S(2)}) %all-to-all-start.7) | async-done | bytes 2752544 | tf_op jit(solution)/shard_map/all_to_all | solution.py:105
  524.7 1.9 broadcast_in_dim_reshape.9
  526.6 2.9 slice.100
  (83 shorter events, 26.4 us)
Async XLA Ops:
  0.6 66.4 %copy-start = (bf16[256,3584]{1,0:T(8,128)(2,1)S(1)}, bf16[256,3584]{1,0:T(8,128)(2,1)}, u32[]{:S(2)}) copy-start(bf16[256,3584]{1,0:T(8,128)(2,1)} %param.14) | copy-start | bytes 5505028
  6.3 7.0 %copy-start.12 = (s32[2]{0:T(128)S(1)}, s32[2]{0:T(128)}, u32[]{:S(2)}) copy-start(s32[2]{0:T(128)} %param.16) | copy-start | bytes 28
  6.3 10.2 %copy-start.10 = (s32[256,4]{0,1:T(4,128)S(1)}, s32[256,4]{0,1:T(4,128)}, u32[]{:S(2)}) copy-start(s32[256,4]{0,1:T(4,128)} %param.12) | copy-start | bytes 12292
  6.3 11.8 %copy-start.13 = (s32[16]{0:T(128)S(1)}, s32[16]{0:T(128)}, u32[]{:S(2)}) copy-start(s32[16]{0:T(128)} %param.17) | copy-start | bytes 196
  6.3 41.1 %all-to-all-start.2 = ((bf16[16,672,128]{2,1,0:T(8,128)(2,1)}), bf16[16,672,128]{2,1,0:T(8,128)(2,1)}, u32[]{:S(2)}, u32[]{:S(2)}) async-start(bf16[16,672,128]{2,1,0:T(8,128)(2,1)} %pad_maximum_fusion), calls=%async_computation.2 | async-start | bytes 5505024 | tf_op jit(solution)/shard_map/all_to_all | solution.py:105
  50.3 39.3 %all-to-all-start.3 = ((bf16[16,672,128]{2,1,0:T(8,128)(2,1)}), bf16[16,672,128]{2,1,0:T(8,128)(2,1)}, u32[]{:S(2)}, u32[]{:S(2)}) async-start(bf16[16,672,128]{2,1,0:T(8,128)(2,1)} %broadcast_select_fusion.2), calls=%async_computation.3 | async-start | bytes 5505024 | tf_op jit(solution)/shard_map/all_to_all | solution.py:105
  82.9 12.1 %copy-start.11 = (f32[256,4]{0,1:T(4,128)S(1)}, f32[256,4]{0,1:T(4,128)}, u32[]{:S(2)}) copy-start(f32[256,4]{0,1:T(4,128)} %param.13) | copy-start | bytes 12292
  89.6 108.5 %all-to-all-start.1 = ((bf16[16,2,40,3584]{3,2,1,0:T(8,128)(2,1)}), bf16[16,2,40,3584]{3,2,1,0:T(8,128)(2,1)}, u32[]{:S(2)}, u32[]{:S(2)}) async-start(bf16[16,2,40,3584]{3,2,1,0:T(8,128)(2,1)} %broadcast_select_fusion), calls=%async_computation.1 | async-start | bytes 18350080 | tf_op jit(solution)/shard_map/all_to_all | solution.py:154
  95.3 5.1 copy-start.2
  198.1 108.6 %all-to-all-start = ((bf16[16,2,40,3584]{3,2,1,0:T(8,128)(2,1)}), bf16[16,2,40,3584]{3,2,1,0:T(8,128)(2,1)}, u32[]{:S(2)}, u32[]{:S(2)}) async-start(bf16[16,2,40,3584]{3,2,1,0:T(8,128)(2,1)} %fusion), calls=%async_computation | async-start | bytes 18350080 | tf_op jit(solution)/shard_map/all_to_all | solution.py:155
  215.0 2.1 copy-start.3
  313.1 1.2 copy-start.9
  313.1 2.5 slice-start
  314.2 1.5 slice-start.1
  319.7 2.1 copy-start.5
  324.7 39.3 %all-to-all-start.4 = ((bf16[16,672,128]{2,1,0:T(8,128)(2,1)}), bf16[16,672,128]{2,1,0:T(8,128)(2,1)}, u32[]{:S(2)}, u32[]{:S(2)}) async-start(bf16[16,672,128]{2,1,0:T(8,128)(2,1)} %pad_maximum_fusion.1), calls=%async_computation.4 | async-start | bytes 5505024 | tf_op jit(solution)/shard_map/all_to_all | solution.py:105
  369.4 5.3 copy-start.4
  369.4 39.4 %all-to-all-start.5 = ((bf16[16,672,128]{2,1,0:T(8,128)(2,1)}), bf16[16,672,128]{2,1,0:T(8,128)(2,1)}, u32[]{:S(2)}, u32[]{:S(2)}) async-start(bf16[16,672,128]{2,1,0:T(8,128)(2,1)} %select_convert_fusion), calls=%async_computation.5 | async-start | bytes 5505024 | tf_op jit(solution)/shard_map/all_to_all | solution.py:105
  381.0 9.2 %slice-start.2 = ((s8[4587520]{0:T(1024)(128)(4,1)}), s8[393216]{0:T(1024)(128)(4,1)S(1)}, s32[]{:S(2)}) async-start(s8[4587520]{0:T(1024)(128)(4,1)} %bitcast.228), calls=%async_computation.10 | async-start | bytes 786432
  385.5 4.6 slice-start.3
  385.5 4.6 copy-start.7
  389.3 0.8 copy-start.14
  419.7 4.9 copy-start.8
  424.5 5.2 copy-start.15
  484.3 39.0 %all-to-all-start.7 = ((bf16[16,672,128]{2,1,0:T(8,128)(2,1)}), bf16[16,672,128]{2,1,0:T(8,128)(2,1)}, u32[]{:S(2)}, u32[]{:S(2)}) async-start(bf16[16,672,128]{2,1,0:T(8,128)(2,1)} %broadcast_select_fusion.1), calls=%async_computation.7 | async-start | bytes 5505024 | tf_op jit(solution)/shard_map/all_to_all | solution.py:105
  491.4 3.9 copy-start.6
  523.3 6.2 %copy-start.1 = (bf16[256,3584]{1,0:T(8,128)(2,1)S(1)}, bf16[256,3584]{1,0:T(8,128)(2,1)}, u32[]{:S(2)}) copy-start(bf16[256,3584]{1,0:T(8,128)(2,1)} %param.14) | copy-start | bytes 5505028
